TPU v7x, 128 devices: a whole 4x4x4 slice. The times are simulated.
128 devices in a mesh: px: 8 (over z, core), py: 16 (over y, x).
Axes of the slice: x: 4, y: 4, z: 4, core: 2. Of those that a mesh axis runs over, the one named last changes fastest.
Arguments:
- fractions: float32 [4096, 3, 128], P(('px', 'py')), may hold values from 0 to 1
- charge: float32 [4096, 128], P(('px', 'py')), may hold values from -4 to 4
- cell_index: int32 [4096, 128], P(('px', 'py')), may hold values from 0 to 131071
- destination: int32 [4096, 1], P(('px', 'py')), may hold values from 0 to 15; in each aligned block of 32 rows (0 to 31, 32 to 63, ...) at most 3 rows name the same one
- live_blocks: int32 [128], P(('px', 'py')), may hold values from 16 to 32, as said below
Outputs:
- forces: float32 [4096, 3, 128], P(('px', 'py'))
Inputs may be any that keep to these rules, and one draw needn't show every extreme that they name: `destination`: in the rows of one device no value is named by more than 3 blocks, a bound that some block reaches. `live_blocks`: some domain has all 32 slots occupied in every draw.
All inputs are finite; a program needn't handle non-finite values.
Results may differ from a plain program's by a relative error of at most 0.0003.
Values sent between devices are 32-bit elements; how exact they have to be, the bound alone decides.
No kernel may reach another device: no remote copies, remote signals or barrier semaphores. Data moves between devices by JAX's collectives and lax.ppermute only.
A program may use at most 128 MiB of HBM per device.

v0:
```python
import math

import jax
import jax.numpy as jnp
from jax import lax
from jax.sharding import PartitionSpec as P

K = 256


EWALD_GAIN = 4.0
EWALD_BETA = 0.6
SPLINE_SUMS = (1.0 / 120.0, 26.0 / 120.0, 66.0 / 120.0, 26.0 / 120.0, 1.0 / 120.0)
HIGHEST = lax.Precision.HIGHEST
HIGH = lax.Precision.HIGH


def swapped(block, axis, bit):
    count = lax.axis_size(axis)
    route = []
    for low in range(count):
        high = low | 1 << bit
        if high != low and high < count:
            route += [(low, high), (high, low)]
    return lax.ppermute(block, axis, route)


def from_behind(value, axis, steps):
    count = lax.axis_size(axis)
    pairs = [(source, (source + steps) % count) for source in range(count)]
    return lax.ppermute(value, axis, pairs)


def from_corner(value, steps):
    rows = lax.axis_size("px")
    cols = lax.axis_size("py")
    pairs = [
        (i * cols + j, (i + steps) % rows * cols + (j + steps) % cols)
        for i in range(rows)
        for j in range(cols)
    ]
    return lax.ppermute(value, ("px", "py"), pairs)


def spline_six(u):
    older_values = [1.0 - u, u]
    slopes = []
    for spline_order in range(3, 7):
        newer_values = []
        for k in range(spline_order):
            from_left = older_values[k - 1] if k >= 1 else jnp.zeros_like(u)
            from_right = older_values[k] if k <= spline_order - 2 else jnp.zeros_like(u)
            newer_values.append(
                ((u + (spline_order - 1 - k)) * from_left + (k + 1 - u) * from_right)
                * (1.0 / (spline_order - 1))
            )
        if spline_order == 6:
            slopes = [
                (older_values[k - 1] if k >= 1 else jnp.zeros_like(u))
                - (older_values[k] if k <= 4 else jnp.zeros_like(u))
                for k in range(6)
            ]
        older_values = newer_values
    return (older_values, slopes)


def modulus(wave, extent):
    cos_sum = jnp.zeros(wave.shape, jnp.float32)
    sin_sum = jnp.zeros(wave.shape, jnp.float32)
    for j, value in enumerate(SPLINE_SUMS):
        angle = 2.0 * math.pi / extent * (wave * j % extent).astype(jnp.float32)
        cos_sum = cos_sum + value * jnp.cos(angle)
        sin_sum = sin_sum + value * jnp.sin(angle)
    return 1.0 / (cos_sum * cos_sum + sin_sum * sin_sum)


def influence(wave_x, wave_y, wave_z, extent):
    folded_x = jnp.where(2 * wave_x < extent, wave_x, wave_x - extent).astype(jnp.float32) / extent
    folded_y = jnp.where(2 * wave_y < extent, wave_y, wave_y - extent).astype(jnp.float32) / extent
    folded_z = jnp.where(2 * wave_z < extent, wave_z, wave_z - extent).astype(jnp.float32) / extent
    squared = folded_x * folded_x + folded_y * folded_y + folded_z * folded_z
    safe_squared = jnp.where(squared > 0, squared, 1.0)
    value = (
        EWALD_GAIN
        * jnp.exp(-(math.pi * math.pi) * squared / (EWALD_BETA * EWALD_BETA))
        / safe_squared
    )
    value = value * modulus(wave_x, extent) * modulus(wave_y, extent) * modulus(wave_z, extent)
    return jnp.where(squared > 0, value, 0.0)


def wave_tables(extent):
    steps = jnp.arange(extent, dtype=jnp.int32)
    product = steps[:, None] * steps[None, :] % extent
    angle = 2.0 * math.pi / extent * product.astype(jnp.float32)
    return (jnp.cos(angle), jnp.sin(angle))


def local_forward(start, count, parts):
    outputs = jnp.arange(count, dtype=jnp.int32)[:, None]
    inputs = jnp.arange(count, dtype=jnp.int32)[None, :]
    total = parts * count
    product = inputs * (start + parts * outputs) % total
    angle = -2.0 * math.pi / total * product.astype(jnp.float32)
    return (jnp.cos(angle), jnp.sin(angle))


def reverse_bits(index, count_bits):
    result = jnp.zeros((), jnp.int32)
    for b in range(count_bits):
        result = result + ((index >> b & 1) << count_bits - 1 - b)
    return result


def mix_rows(spectrum, mat_cos, mat_sin):

    def apply_matrix(matrix, values):
        return jnp.einsum("sm,myz->syz", matrix, values, precision=HIGH)

    real_part, imag_part = (spectrum[0], spectrum[1])
    return jnp.stack(
        [
            apply_matrix(mat_cos, real_part) - apply_matrix(mat_sin, imag_part),
            apply_matrix(mat_cos, imag_part) + apply_matrix(mat_sin, real_part),
        ]
    )


def mix_columns(spectrum, mat_cos, mat_sin):

    def apply_matrix(matrix, values):
        return jnp.einsum("sm,xmz->xsz", matrix, values, precision=HIGH)

    real_part, imag_part = (spectrum[0], spectrum[1])
    return jnp.stack(
        [
            apply_matrix(mat_cos, real_part) - apply_matrix(mat_sin, imag_part),
            apply_matrix(mat_cos, imag_part) + apply_matrix(mat_sin, real_part),
        ]
    )


def swap_rows(spectrum, bit_number):
    return swapped(spectrum, "px", bit_number)


def swap_columns(spectrum, bit_number):
    return swapped(spectrum, "py", bit_number)


def butterfly_section(spectrum, index, bit_number, inverse, exchanger):
    upper = index >> bit_number & 1 == 1
    lower = (index & (1 << bit_number) - 1).astype(jnp.float32)
    angle = -2.0 * math.pi / 2 ** (bit_number + 1) * lower
    turn_cos = jnp.cos(angle)
    turn_sin = jnp.sin(angle)
    real_part, imag_part = (spectrum[0], spectrum[1])
    if inverse:
        turned = jnp.stack(
            [
                turn_cos * real_part + turn_sin * imag_part,
                turn_cos * imag_part - turn_sin * real_part,
            ]
        )
        own_value = jnp.where(upper, turned, spectrum)
        partner = exchanger(own_value, bit_number)
        return jnp.where(upper, partner - own_value, own_value + partner)
    partner = exchanger(spectrum, bit_number)
    diff_real = partner[0] - real_part
    diff_imag = partner[1] - imag_part
    turned = jnp.stack(
        [turn_cos * diff_real - turn_sin * diff_imag, turn_sin * diff_real + turn_cos * diff_imag]
    )
    return jnp.where(upper, turned, spectrum + partner)


def complex_turn(apply_matrix, spectrum, mat_cos, mat_sin, inverse):
    real_part, imag_part = (spectrum[0], spectrum[1])
    sign = 1.0 if inverse else -1.0
    return jnp.stack(
        [
            apply_matrix(mat_cos, real_part) - sign * apply_matrix(mat_sin, imag_part),
            apply_matrix(mat_cos, imag_part) + sign * apply_matrix(mat_sin, real_part),
        ]
    )


def transform_rows(spectrum, mat_cos, mat_sin, inverse):

    def apply_matrix(matrix, values):
        return jnp.einsum("sm,myz->syz", matrix, values, precision=HIGH)

    return complex_turn(apply_matrix, spectrum, mat_cos, mat_sin, inverse)


def transform_columns(spectrum, mat_cos, mat_sin, inverse):

    def apply_matrix(matrix, values):
        return jnp.einsum("sm,xmz->xsz", matrix, values, precision=HIGH)

    return complex_turn(apply_matrix, spectrum, mat_cos, mat_sin, inverse)


def complex_block(mat_cos, mat_sin, inverse):
    turn_imag = mat_sin if inverse else -mat_sin
    return jnp.stack([jnp.stack([mat_cos, -turn_imag]), jnp.stack([turn_imag, mat_cos])])


def place_table(base, values, span):
    atoms_count = base.shape[0]
    slots_index = jnp.arange(span, dtype=jnp.int32)[:, None]
    table = jnp.zeros((span, atoms_count), jnp.float32)
    for k in range(6):
        table = table + jnp.where(slots_index == (base + k)[None, :], values[k][None, :], 0.0)
    return table


def place_depth(base, values, extent):
    depth_index = jnp.arange(extent, dtype=jnp.int32)[None, :]
    table = jnp.zeros((base.shape[0], extent), jnp.float32)
    for k in range(6):
        table = table + jnp.where(
            depth_index == ((base + k) % extent)[:, None], values[k][:, None], 0.0
        )
    return table


def per_device(fractions, charge, cell_index, destination, live_blocks):
    rows_dev = lax.axis_size("px")
    cols_dev = lax.axis_size("py")
    span_x = K // rows_dev
    span_y = K // cols_dev
    blocks = charge.shape[0]
    width = charge.shape[1]
    capacity = max(2, 3 * blocks // (2 * cols_dev))
    slots = cols_dev * capacity
    alive = (jnp.arange(blocks, dtype=jnp.int32) < live_blocks[0]).astype(jnp.float32)
    target = destination[:, 0]
    matches = (target[:, None] == jnp.arange(cols_dev, dtype=jnp.int32)[None, :]).astype(jnp.int32)
    earlier = jnp.cumsum(matches, axis=0) - matches
    position = jnp.sum(earlier * matches, axis=1)
    slot_of = target * capacity + position
    picked = (slot_of[None, :] == jnp.arange(slots, dtype=jnp.int32)[:, None]).astype(jnp.int32)
    source_block = jnp.sum(picked * jnp.arange(blocks, dtype=jnp.int32)[None, :], axis=1)
    used = jnp.sum(picked, axis=1).astype(jnp.float32)
    payload = jnp.concatenate(
        [
            fractions,
            (charge * alive[:, None])[:, None, :],
            cell_index.astype(jnp.float32)[:, None, :],
        ],
        axis=1,
    )
    outgoing = (jnp.take(payload, source_block, axis=0) * used[:, None, None]).reshape(
        cols_dev, capacity, 5, width
    )
    arrived = lax.all_to_all(outgoing, "py", split_axis=0, concat_axis=0, tiled=True)
    atoms = slots * width
    placed = arrived.reshape(slots, 5, width).transpose(1, 0, 2).reshape(5, atoms)
    cell_value = placed[4].astype(jnp.int32)
    amounts = placed[3]
    base_x = cell_value // (span_y * K)
    base_y = cell_value // K % span_y
    base_z = cell_value % K
    splines_x, slopes_x = spline_six(placed[0])
    splines_y, slopes_y = spline_six(placed[1])
    splines_z, slopes_z = spline_six(placed[2])
    table_x = place_table(base_x, splines_x, span_x + 5)
    slope_x = place_table(base_x, slopes_x, span_x + 5)
    pad_y = -(-(span_y + 5) // 8) * 8
    table_y = place_table(base_y, splines_y, pad_y)
    slope_y = place_table(base_y, slopes_y, pad_y)
    both_z = place_depth(
        jnp.concatenate([base_z, base_z]),
        [jnp.concatenate([splines_z[k], slopes_z[k]]) for k in range(6)],
        K,
    )
    both_z = lax.optimization_barrier(both_z)
    outer_table = ((table_x * amounts[None, :])[:, None, :] * table_y[None, :, :]).reshape(-1, atoms)
    extended = jnp.dot(outer_table, both_z[:atoms], precision=HIGH)
    extended = extended.reshape(span_x + 5, pad_y, K)
    moved_rows = from_behind(extended[span_x:, :span_y], "px", 1)
    moved_cols = from_behind(extended[:span_x, span_y : span_y + 5], "py", 1)
    moved_corner = from_corner(extended[span_x:, span_y : span_y + 5], 1)
    charge_grid = extended[:span_x, :span_y]
    charge_grid = charge_grid.at[:5].add(moved_rows)
    charge_grid = charge_grid.at[:, :5].add(moved_cols)
    charge_grid = charge_grid.at[:5, :5].add(moved_corner)
    index_x = lax.axis_index("px")
    index_y = lax.axis_index("py")
    span_ky = K // rows_dev
    span_kz = K // cols_dev
    wave_cos, wave_sin = wave_tables(K)
    ahead_z = jnp.stack([wave_cos, -wave_sin]).reshape(2, cols_dev, span_kz, K)
    flat_grid = charge_grid.reshape(span_x * span_y, K)
    spectrum = jnp.einsum("cjkz,mz->jckm", ahead_z, flat_grid, precision=HIGH)
    spectrum = lax.all_to_all(spectrum, "py", 0, 0, tiled=True)
    spectrum = spectrum.reshape(cols_dev, 2, span_kz, span_x, span_y)
    turn_y = complex_block(wave_cos, wave_sin, False).reshape(2, 2, rows_dev, span_ky, cols_dev, span_y)
    spectrum = jnp.einsum("dcilsy,sckxy->idlkx", turn_y, spectrum, precision=HIGH)
    spectrum = spectrum.reshape(rows_dev, 2, span_ky, span_kz * span_x)
    spectrum = lax.all_to_all(spectrum, "px", 0, 0, tiled=True)
    spectrum = spectrum.reshape(rows_dev, 2, span_ky, span_kz, span_x)
    turn_x = complex_block(wave_cos, wave_sin, False).reshape(2, 2, K, rows_dev, span_x)
    spectrum = jnp.einsum("dcqrx,rclkx->qdlk", turn_x, spectrum, precision=HIGH)
    wave_x = jnp.arange(K, dtype=jnp.int32)
    wave_y = index_x * span_ky + jnp.arange(span_ky, dtype=jnp.int32)
    wave_z = index_y * span_kz + jnp.arange(span_kz, dtype=jnp.int32)
    kernel = influence(wave_x[:, None, None], wave_y[None, :, None], wave_z[None, None, :], K) * (
        1.0 / float(K**3)
    )
    spectrum = spectrum * kernel[:, None]
    back_x = complex_block(wave_cos, wave_sin, True).reshape(2, 2, rows_dev, span_x, K)
    spectrum = jnp.einsum("dcrxq,qclk->rdlkx", back_x, spectrum, precision=HIGH)
    spectrum = spectrum.reshape(rows_dev, 2, span_ky, span_kz * span_x)
    spectrum = lax.all_to_all(spectrum, "px", 0, 0, tiled=True)
    spectrum = spectrum.reshape(rows_dev, 2, span_ky, span_kz, span_x)
    back_y = complex_block(wave_cos, wave_sin, True).reshape(2, 2, cols_dev, span_y, rows_dev, span_ky)
    spectrum = jnp.einsum("dcsyil,iclkx->sdkxy", back_y, spectrum, precision=HIGH)
    spectrum = spectrum.reshape(cols_dev, 2, span_kz, span_x * span_y)
    spectrum = lax.all_to_all(spectrum, "py", 0, 0, tiled=True)
    back_z = jnp.stack([wave_cos, -wave_sin], axis=1).reshape(K, 2, cols_dev, span_kz)
    potential = jnp.einsum("zcjk,jckm->mz", back_z, spectrum, precision=HIGH)
    potential = potential.reshape(span_x, span_y, K)
    lower_rows = from_behind(potential[:5], "px", -1)
    lower_cols = from_behind(potential[:, :5], "py", -1)
    lower_corner = from_corner(potential[:5, :5], -1)
    gap = jnp.zeros((span_x + 5, pad_y - span_y - 5, K), jnp.float32)
    potential = jnp.concatenate(
        [
            jnp.concatenate([potential, lower_rows], axis=0),
            jnp.concatenate([lower_cols, lower_corner], axis=0),
            gap,
        ],
        axis=1,
    ).reshape(-1, K)
    potential = lax.optimization_barrier(potential)

    sampled = lax.dot_general(
        potential, both_z, (((1,), (1,)), ((), ())), precision=HIGH
    ).reshape(span_x + 5, pad_y, 2, atoms)
    plain = sampled[:, :, 0]
    sloped = sampled[:, :, 1]
    force_x = jnp.sum(slope_x[:, None, :] * table_y[None, :, :] * plain, axis=(0, 1))
    force_y = jnp.sum(table_x[:, None, :] * slope_y[None, :, :] * plain, axis=(0, 1))
    force_z = jnp.sum(table_x[:, None, :] * table_y[None, :, :] * sloped, axis=(0, 1))
    pulled = (-amounts[None, :] * jnp.stack([force_x, force_y, force_z])).reshape(3, slots, width)
    pulled = pulled.transpose(1, 0, 2).reshape(cols_dev, capacity, 3, width)
    returned = lax.all_to_all(pulled, "py", split_axis=0, concat_axis=0, tiled=True).reshape(
        slots, 3, width
    )
    return jnp.take(returned, slot_of, axis=0) * alive[:, None, None]


def solution(mesh):
    placed = (
        P(("px", "py"), None, None),
        P(("px", "py"), None),
        P(("px", "py"), None),
        P(("px", "py"), None),
        P(("px", "py")),
    )
    return jax.shard_map(
        per_device,
        mesh=mesh,
        in_specs=placed,
        out_specs=P(("px", "py"), None, None),
        check_vma=False,
    )
```

profile of v0, /device:TPU:0, one launch (start us, length us, event | category | flops | bytes accessed | tf_op | source)
XLA Modules:
  0.0 425.2 jit_solution(14916240516073902117)
XLA Ops:
  7.1 7.1 %all-to-all-start = ((f32[16,3,5,128]{3,1,2,0:T(4,128)}), f32[16,3,5,128]{3,1,2,0:T(4,128)S(1)}, u32[]{:S(2)}, u32[]{:S(2)}) async-start(f32[16,3,5,128]{3,1,2,0:T(4,128)} %copy.63), calls=%async_computation | async-start | bytes 327680 | tf_op jit(solution)/shard_map/all_to_all | solution.py:257
  14.3 8.2 %all-to-all-done = f32[16,3,5,128]{3,1,2,0:T(4,128)S(1)} async-done(((f32[16,3,5,128]{3,1,2,0:T(4,128)}), f32[16,3,5,128]{3,1,2,0:T(4,128)S(1)}, u32[]{:S(2)}, u32[]{:S(2)}) %all-to-all-start) | async-done | bytes 122912 | tf_op jit(solution)/shard_map/all_to_all | solution.py:257
  23.7 19.9 %select_add_fusion = f32[12288,256]{1,0:T(8,128)S(1)} fusion(f32[12288]{0:T(1024)S(1)} %get-tuple-element.145, s32[12288]{0:T(1024)S(1)} %get-tuple-element.111, f32[12288]{0:T(1024)S(1)} %get-tuple-element.144, s32[12288]{0:T(1024)S(1)} %get-tuple-element.112, f32[12288]{0:T(1024)S(1)} %get-tuple-element.143, s32[12288]{0:T(1024)S(1)} %get-tuple-element.115, ...), kind=kLoop, calls=%fused_computation.10 | loop fusion | flops 53477376 | bytes 13172736 | tf_op jit(solution)/shard_map/add | solution.py:222
  48.2 8.8 %fusion.2 = f32[37,24,256]{2,1,0:T(8,128)S(1)} fusion(f32[37,6144]{1,0:T(8,128)S(1)} %get-tuple-element.64, f32[24,6144]{1,0:T(8,128)S(1)} %get-tuple-element.67, f32[12288,256]{1,0:T(8,128)S(1)} %select_add_fusion), kind=kOutput, calls=%fused_computation.8 | convolution fusion | flops 8385675264 | bytes 8773632 | tf_op jit(solution)/shard_map/dot_general | solution.py:280
  62.1 7.7 %collective-permute-done.1 = f32[32,5,256]{2,1,0:T(8,128)S(1)} collective-permute-done((f32[32,5,256]{2,1,0:T(8,128)S(1)}, f32[32,5,256]{2,1,0:T(8,128)S(1)}, u32[]{:S(2)}, u32[]{:S(2)}) %collective-permute-start.1) | collective-permute-done | bytes 163872 | tf_op jit(solution)/shard_map/ppermute | solution.py:31
  73.7 3.7 all-to-all-start.1
  77.7 5.9 %fusion.63 = (f32[1,1,8,32,16,16]{3,5,4,1,2,0:T(8,128)S(1)}, f32[1,1,8,32,16,16]{3,5,4,1,2,0:T(8,128)}, f32[1,1,8,32,16,16]{3,5,4,1,2,0:T(8,128)}) fusion(s32[16,16]{1,0:T(8,128)S(1)} %multiply_add_fusion, s32[8,32]{1,0:T(8,128)S(1)} %multiply_add_fusion.1), kind=kLoop, calls=%fused_computation.110 | loop fusion | flops 983040 | bytes 788480 | tf_op jit(solution)/shard_map/sin | solution.py:96
  83.6 11.6 %all-to-all-done.1 = f32[16,2,16,512]{3,2,1,0:T(8,128)S(1)} async-done(((f32[16,2,16,512]{3,2,1,0:T(8,128)}), f32[16,2,16,512]{3,2,1,0:T(8,128)S(1)}, u32[]{:S(2)}, u32[]{:S(2)}) %all-to-all-start.1) | async-done | bytes 1048608 | tf_op jit(solution)/shard_map/all_to_all | solution.py:297
  95.2 4.8 %reshape.2976 = f32[16,2,16,32,16]{4,3,2,1,0:T(8,128)} reshape(f32[16,2,16,512]{3,2,1,0:T(8,128)S(1)} %all-to-all-done.1) | data formatting | bytes 2097152 | tf_op jit(solution)/shard_map/reshape | solution.py:298
  100.0 19.0 %fusion.27 = f32[8,2,32,16,32]{2,4,0,1,3:T(8,128)} fusion(f32[1,1,8,32,16,16]{3,5,4,1,2,0:T(8,128)} %get-tuple-element.126, f32[1,1,8,32,16,16]{3,5,4,1,2,0:T(8,128)} %get-tuple-element.125, f32[1,1,8,32,16,16]{3,5,4,1,2,0:T(8,128)S(1)} %get-tuple-element.124, f32[16,2,16,32,16]{4,3,2,1,0:T(8,128)} %reshape.2976), kind=kOutput, calls=%fused_computation.41 | convolution fusion | flops 806092800 | bytes 2883584 | tf_op jit(solution)/shard_map/dcilsy,sckxy->idlkx/dot_general | solution.py:300
  119.0 5.6 %copy.67 = f32[8,2,32,16,32]{4,3,2,1,0:T(8,128)} copy(f32[8,2,32,16,32]{2,4,0,1,3:T(8,128)} %fusion.27) | data formatting | bytes 2097152 | tf_op jit(solution)/shard_map/dcilsy,sckxy->idlkx/transpose | solution.py:300
  124.6 4.4 %reshape.2977 = f32[8,2,32,512]{3,2,1,0:T(8,128)} reshape(f32[8,2,32,16,32]{4,3,2,1,0:T(8,128)} %copy.67) | data formatting | bytes 2097152 | tf_op jit(solution)/shard_map/reshape | solution.py:301
  129.0 6.6 %all-to-all-start.2 = ((f32[8,2,32,512]{3,2,1,0:T(8,128)}), f32[8,2,32,512]{3,2,1,0:T(8,128)S(1)}, u32[]{:S(2)}, u32[]{:S(2)}) async-start(f32[8,2,32,512]{3,2,1,0:T(8,128)} %reshape.2977), calls=%async_computation.2 | async-start | bytes 2097152 | tf_op jit(solution)/shard_map/all_to_all | solution.py:302
  140.8 10.7 %all-to-all-done.2 = f32[8,2,32,512]{3,2,1,0:T(8,128)S(1)} async-done(((f32[8,2,32,512]{3,2,1,0:T(8,128)}), f32[8,2,32,512]{3,2,1,0:T(8,128)S(1)}, u32[]{:S(2)}, u32[]{:S(2)}) %all-to-all-start.2) | async-done | bytes 1048608 | tf_op jit(solution)/shard_map/all_to_all | solution.py:302
  155.4 4.5 %fusion.22 = f32[32,16,2,256,1,1]{3,1,4,2,0,5:T(8,128)S(1)} fusion(f32[8,2,32,16,32,1]{4,3,1,2,0,5:T(8,128)} %reshape.3008, f32[1,1,256,8,32]{2,4,3,1,0:T(8,128)} %get-tuple-element.136, f32[1,1,256,8,32]{2,4,3,1,0:T(8,128)} %get-tuple-element.135, f32[1,1,256,8,32]{2,4,3,1,0:T(8,128)} %get-tuple-element.134), kind=kOutput, calls=%fused_computation.38 | convolution fusion | flops 806092800 | bytes 2883584 | tf_op jit(solution)/shard_map/dcqrx,rclkx->qdlk/dot_general | solution.py:305
  159.9 5.0 %convolution_bitcast_fusion = f32[8,2,32,16,32]{4,3,0,1,2:T(8,128)} fusion(f32[1,1,8,32,256]{4,3,1,2,0:T(8,128)S(1)} %copy-done.7, f32[1,1,8,32,256]{4,3,1,2,0:T(8,128)S(1)} %copy-done.6, f32[1,1,8,32,256]{4,3,1,2,0:T(8,128)S(1)} %get-tuple-element.137, f32[32,16,2,256,1,1]{3,1,4,2,0,5:T(8,128)S(1)} %fusion.22, f32[256,32,16]{0,2,1:T(8,128)S(1)} %copy-done.5), kind=kOutput, calls=%fused_computation.42 | convolution fusion | flops 806354944 | bytes 3407872 | tf_op jit(solution)/shard_map/dcrxq,qclk->rdlkx/dot_general | solution.py:314
  164.9 3.5 reshape.2979
  170.0 3.8 all-to-all-start.3
  173.8 5.8 %fusion.66 = (f32[1,1,16,16,8,32]{5,3,4,1,2,0:T(8,128)S(1)}, f32[1,1,16,16,8,32]{5,3,4,1,2,0:T(8,128)}, f32[1,1,16,16,8,32]{5,3,4,1,2,0:T(8,128)}) fusion(s32[8,32]{1,0:T(8,128)S(1)} %multiply_add_fusion.1, s32[16,16]{1,0:T(8,128)S(1)} %multiply_add_fusion), kind=kLoop, calls=%fused_computation.126 | loop fusion | flops 983040 | bytes 788480 | tf_op jit(solution)/shard_map/neg | solution.py:294
  179.6 10.0 %all-to-all-done.3 = f32[8,2,32,512]{3,2,1,0:T(8,128)S(1)} async-done(((f32[8,2,32,512]{3,2,1,0:T(8,128)}), f32[8,2,32,512]{3,2,1,0:T(8,128)S(1)}, u32[]{:S(2)}, u32[]{:S(2)}) %all-to-all-start.3) | async-done | bytes 1048608 | tf_op jit(solution)/shard_map/all_to_all | solution.py:316
  192.1 11.0 %fusion.24 = f32[16,2,16,32,16]{3,4,0,1,2:T(8,128)} fusion(f32[1,1,16,16,8,32]{5,3,4,1,2,0:T(8,128)} %get-tuple-element.129, f32[1,1,16,16,8,32]{5,3,4,1,2,0:T(8,128)} %get-tuple-element.128, f32[1,1,16,16,8,32]{5,3,4,1,2,0:T(8,128)S(1)} %get-tuple-element.127, f32[8,2,32,16,32,1,1]{4,3,2,1,0,6,5:T(8,128)} %bitcast.317), kind=kOutput, calls=%fused_computation.40 | convolution fusion | flops 806092800 | bytes 2883584 | tf_op jit(solution)/shard_map/dcsyil,iclkx->sdkxy/dot_general | solution.py:319
  203.1 7.0 %copy.73 = f32[16,2,16,32,16]{4,3,2,1,0:T(8,128)} copy(f32[16,2,16,32,16]{3,4,0,1,2:T(8,128)} %fusion.24) | data formatting | bytes 2097152 | tf_op jit(solution)/shard_map/dcsyil,iclkx->sdkxy/transpose | solution.py:319
  210.1 8.3 %reshape.2981 = f32[16,2,16,512]{3,2,1,0:T(8,128)} reshape(f32[16,2,16,32,16]{4,3,2,1,0:T(8,128)} %copy.73) | data formatting | bytes 2097152 | tf_op jit(solution)/shard_map/reshape | solution.py:320
  218.4 3.7 all-to-all-start.4
  223.2 16.5 %all-to-all-done.4 = f32[16,2,16,512]{3,2,1,0:T(8,128)S(1)} async-done(((f32[16,2,16,512]{3,2,1,0:T(8,128)}), f32[16,2,16,512]{3,2,1,0:T(8,128)S(1)}, u32[]{:S(2)}, u32[]{:S(2)}) %all-to-all-start.4) | async-done | bytes 1048608 | tf_op jit(solution)/shard_map/all_to_all | solution.py:321
  243.6 3.2 collective-permute-done.5
  247.8 32.4 %fusion.236 = f32[888,12288]{1,0:T(8,128)} fusion(f32[888,256]{1,0:T(8,128)S(1)} %bitcast.318, f32[12288,256]{1,0:T(8,128)} %copy-done), kind=kOutput, calls=%fused_computation.480 | convolution fusion | flops 16760438784 | bytes 57139200 | tf_op jit(solution)/shard_map/dot_general | solution.py:339
  280.2 53.2 %reshape.2984 = f32[37,24,2,6144]{3,2,1,0:T(2,128)} reshape(f32[888,12288]{1,0:T(8,128)} %fusion.236) | data formatting | bytes 87293952 | tf_op jit(solution)/shard_map/reshape | solution.py:341
  333.4 43.7 %fusion.235 = (f32[37,24,1,6144]{3,2,1,0:T(1,128)}, f32[37,24,1,6144]{3,2,1,0:T(1,128)}) fusion(f32[37,24,2,6144]{3,2,1,0:T(2,128)} %reshape.2984), kind=kLoop, calls=%fused_computation.479 | loop fusion | bytes 87293952 | tf_op jit(solution)/shard_map/slice | solution.py:343
  377.2 31.6 %multiply_reduce_fusion.1 = (f32[6144]{0:T(1024)S(1)}, f32[6144]{0:T(1024)S(1)}, f32[6144]{0:T(1024)S(1)}) fusion(f32[37,24,1,6144]{3,2,1,0:T(1,128)} %get-tuple-element.62, f32[24,6144]{1,0:T(8,128)S(1)} %copy-done.4, f32[37,6144]{1,0:T(8,128)S(1)} %copy-done.1, f32[24,6144]{1,0:T(8,128)S(1)} %copy-done.2, f32[37,6144]{1,0:T(8,128)S(1)} %get-tuple-element.63, ...), kind=kLoop, calls=%fused_computation.7 | loop fusion | flops 49084416 | bytes 46718976 | tf_op jit(solution)/shard_map/reduce_sum | solution.py:344
  409.6 5.9 %all-to-all-start.5 = ((f32[16,3,3,128]{3,1,2,0:T(4,128)}), f32[16,3,3,128]{3,1,2,0:T(4,128)S(1)}, u32[]{:S(2)}, u32[]{:S(2)}) async-start(f32[16,3,3,128]{3,1,2,0:T(4,128)} %copy.77), calls=%async_computation.5 | async-start | bytes 196608 | tf_op jit(solution)/shard_map/all_to_all | solution.py:349
  415.5 7.8 %all-to-all-done.5 = f32[16,3,3,128]{3,1,2,0:T(4,128)S(1)} async-done(((f32[16,3,3,128]{3,1,2,0:T(4,128)}), f32[16,3,3,128]{3,1,2,0:T(4,128)S(1)}, u32[]{:S(2)}, u32[]{:S(2)}) %all-to-all-start.5) | async-done | bytes 73760 | tf_op jit(solution)/shard_map/all_to_all | solution.py:349
  (113 shorter events, 42.4 us)
Async XLA Ops:
  3.1 2.5 copy-start.10
  7.1 15.3 %all-to-all-start = ((f32[16,3,5,128]{3,1,2,0:T(4,128)}), f32[16,3,5,128]{3,1,2,0:T(4,128)S(1)}, u32[]{:S(2)}, u32[]{:S(2)}) async-start(f32[16,3,5,128]{3,1,2,0:T(4,128)} %copy.63), calls=%async_computation | async-start | bytes 327680 | tf_op jit(solution)/shard_map/all_to_all | solution.py:257
  43.6 13.3 %copy-start = (f32[12288,256]{1,0:T(8,128)}, f32[12288,256]{1,0:T(8,128)S(1)}, u32[]{:S(2)}) copy-start(f32[12288,256]{1,0:T(8,128)S(1)} %select_add_fusion) | copy-start | bytes 37748740
  45.6 11.4 %copy-start.3 = (f32[24,6144]{1,0:T(8,128)}, f32[24,6144]{1,0:T(8,128)S(1)}, u32[]{:S(2)}) copy-start(f32[24,6144]{1,0:T(8,128)S(1)} %get-tuple-element.67) | copy-start | bytes 1769476
  57.0 5.1 %collective-permute-start = (f32[5,16,256]{2,1,0:T(8,128)S(1)}, f32[5,16,256]{2,1,0:T(8,128)S(1)}, u32[]{:S(2)}, u32[]{:S(2)}) collective-permute-start(f32[5,16,256]{2,1,0:T(8,128)S(1)} %slice.162), channel_id=1, source_target_pairs={{0,16},{16,32},{32,48},{48,64},{64,80},{80,96},{96,112},{112,0},{1... | collective-permute-start | bytes 245768 | tf_op jit(solution)/shard_map/ppermute | solution.py:31
  58.3 11.5 %collective-permute-start.1 = (f32[32,5,256]{2,1,0:T(8,128)S(1)}, f32[32,5,256]{2,1,0:T(8,128)S(1)}, u32[]{:S(2)}, u32[]{:S(2)}) collective-permute-start(f32[32,5,256]{2,1,0:T(8,128)S(1)} %slice.164), channel_id=1, source_target_pairs={{0,1},{1,2},{2,3},{3,4},{4,5},{5,6},{6,7},{7,8},{8,9},{9,10},{10,1... | collective-permute-start | bytes 491528 | tf_op jit(solution)/shard_map/ppermute | solution.py:31
  58.9 13.0 %collective-permute-start.2 = (f32[5,5,256]{2,1,0:T(8,128)S(1)}, f32[5,5,256]{2,1,0:T(8,128)S(1)}, u32[]{:S(2)}, u32[]{:S(2)}) collective-permute-start(f32[5,5,256]{2,1,0:T(8,128)S(1)} %slice.166), channel_id=1, source_target_pairs={{0,17},{1,18},{2,19},{3,20},{4,21},{5,22},{6,23},{7,24},{8,25},{9,... | collective-permute-start | bytes 76808 | tf_op jit(solution)/shard_map/ppermute | solution.py:42
  73.7 21.5 %all-to-all-start.1 = ((f32[16,2,16,512]{3,2,1,0:T(8,128)}), f32[16,2,16,512]{3,2,1,0:T(8,128)S(1)}, u32[]{:S(2)}, u32[]{:S(2)}) async-start(f32[16,2,16,512]{3,2,1,0:T(8,128)} %copy.65), calls=%async_computation.1 | async-start | bytes 2097152 | tf_op jit(solution)/shard_map/all_to_all | solution.py:297
  129.0 22.5 %all-to-all-start.2 = ((f32[8,2,32,512]{3,2,1,0:T(8,128)}), f32[8,2,32,512]{3,2,1,0:T(8,128)S(1)}, u32[]{:S(2)}, u32[]{:S(2)}) async-start(f32[8,2,32,512]{3,2,1,0:T(8,128)} %reshape.2977), calls=%async_computation.2 | async-start | bytes 2097152 | tf_op jit(solution)/shard_map/all_to_all | solution.py:302
  152.3 7.5 %copy-start.5 = (f32[256,32,16]{0,2,1:T(8,128)S(1)}, f32[256,32,16]{0,2,1:T(8,128)}, u32[]{:S(2)}) copy-start(f32[256,32,16]{0,2,1:T(8,128)} %fusion.48) | copy-start | bytes 1572868
  152.4 7.5 %copy-start.6 = (f32[1,1,8,32,256]{4,3,1,2,0:T(8,128)S(1)}, f32[1,1,8,32,256]{4,3,1,2,0:T(8,128)}, u32[]{:S(2)}) copy-start(f32[1,1,8,32,256]{4,3,1,2,0:T(8,128)} %get-tuple-element.138) | copy-start | bytes 786436
  152.4 7.5 %copy-start.7 = (f32[1,1,8,32,256]{4,3,1,2,0:T(8,128)S(1)}, f32[1,1,8,32,256]{4,3,1,2,0:T(8,128)}, u32[]{:S(2)}) copy-start(f32[1,1,8,32,256]{4,3,1,2,0:T(8,128)} %get-tuple-element.139) | copy-start | bytes 786436
  170.0 19.6 %all-to-all-start.3 = ((f32[8,2,32,512]{3,2,1,0:T(8,128)}), f32[8,2,32,512]{3,2,1,0:T(8,128)S(1)}, u32[]{:S(2)}, u32[]{:S(2)}) async-start(f32[8,2,32,512]{3,2,1,0:T(8,128)} %copy.71), calls=%async_computation.3 | async-start | bytes 2097152 | tf_op jit(solution)/shard_map/all_to_all | solution.py:316
  210.1 33.4 %copy-start.9 = (s32[32,1]{0,1:T(1,128)S(1)}, s32[32,1]{0,1:T(1,128)}, u32[]{:S(2)}) copy-start(s32[32,1]{0,1:T(1,128)} %param.14) | copy-start | bytes 388
  218.4 21.3 %all-to-all-start.4 = ((f32[16,2,16,512]{3,2,1,0:T(8,128)}), f32[16,2,16,512]{3,2,1,0:T(8,128)S(1)}, u32[]{:S(2)}, u32[]{:S(2)}) async-start(f32[16,2,16,512]{3,2,1,0:T(8,128)} %reshape.2981), calls=%async_computation.4 | async-start | bytes 2097152 | tf_op jit(solution)/shard_map/all_to_all | solution.py:321
  240.7 6.9 %collective-permute-start.4 = (f32[32,5,256]{2,1,0:T(8,128)S(1)}, f32[32,5,256]{2,1,0:T(8,128)S(1)}, u32[]{:S(2)}, u32[]{:S(2)}) collective-permute-start(f32[32,5,256]{2,1,0:T(8,128)S(1)} %slice.168), channel_id=1, source_target_pairs={{0,15},{1,0},{2,1},{3,2},{4,3},{5,4},{6,5},{7,6},{8,7},{9,8},{10,9... | collective-permute-start | bytes 491528 | tf_op jit(solution)/shard_map/ppermute | solution.py:31
  241.7 5.1 %collective-permute-start.3 = (f32[5,16,256]{2,1,0:T(8,128)S(1)}, f32[5,16,256]{2,1,0:T(8,128)S(1)}, u32[]{:S(2)}, u32[]{:S(2)}) collective-permute-start(f32[5,16,256]{2,1,0:T(8,128)S(1)} %bitcast.337), channel_id=1, source_target_pairs={{0,112},{16,0},{32,16},{48,32},{64,48},{80,64},{96,80},{112,96},{1... | collective-permute-start | bytes 245768 | tf_op jit(solution)/shard_map/ppermute | solution.py:31
  241.7 5.1 %collective-permute-start.5 = (f32[5,5,256]{2,1,0:T(8,128)S(1)}, f32[5,5,256]{2,1,0:T(8,128)S(1)}, u32[]{:S(2)}, u32[]{:S(2)}) collective-permute-start(f32[5,5,256]{2,1,0:T(8,128)S(1)} %slice.169), channel_id=1, source_target_pairs={{0,127},{1,112},{2,113},{3,114},{4,115},{5,116},{6,117},{7,118},{8... | collective-permute-start | bytes 76808 | tf_op jit(solution)/shard_map/ppermute | solution.py:42
  333.4 43.7 %copy-start.1 = (f32[37,6144]{1,0:T(8,128)S(1)}, f32[37,6144]{1,0:T(8,128)}, u32[]{:S(2)}) copy-start(f32[37,6144]{1,0:T(8,128)} %get-tuple-element.65) | copy-start | bytes 2727940
  333.4 43.7 %copy-start.2 = (f32[24,6144]{1,0:T(8,128)S(1)}, f32[24,6144]{1,0:T(8,128)}, u32[]{:S(2)}) copy-start(f32[24,6144]{1,0:T(8,128)} %get-tuple-element.66) | copy-start | bytes 1769476
  333.4 43.7 %copy-start.4 = (f32[24,6144]{1,0:T(8,128)S(1)}, f32[24,6144]{1,0:T(8,128)}, u32[]{:S(2)}) copy-start(f32[24,6144]{1,0:T(8,128)} %copy-done.3) | copy-start | bytes 1769476
  377.2 31.7 %copy-start.8 = (f32[48,128]{1,0:T(8,128)S(1)}, f32[48,128]{1,0:T(8,128)}, u32[]{:S(2)}) copy-start(f32[48,128]{1,0:T(8,128)} %get-tuple-element.77) | copy-start | bytes 73732
  377.2 46.8 %copy-start.11 = (f32[32]{0:T(128)S(1)}, f32[32]{0:T(128)}, u32[]{:S(2)}) copy-start(f32[32]{0:T(128)} %copy-done.10) | copy-start | bytes 388
  409.6 13.8 %all-to-all-start.5 = ((f32[16,3,3,128]{3,1,2,0:T(4,128)}), f32[16,3,3,128]{3,1,2,0:T(4,128)S(1)}, u32[]{:S(2)}, u32[]{:S(2)}) async-start(f32[16,3,3,128]{3,1,2,0:T(4,128)} %copy.77), calls=%async_computation.5 | async-start | bytes 196608 | tf_op jit(solution)/shard_map/all_to_all | solution.py:349
where the time goes:
time: 433 us; the launch traced here: 425 us
  local copies, waits for them, and re-layouts  144 us (33%)
  matrix products  82.3 us (19%)
  other arithmetic  81.7 us (19%)
  waiting for transfers between devices  79.1 us (18%)
  starting transfers between devices  36.4 us (8%)
    reshape x1, local copies, waits for them, and re-layouts, per_device(): sampled = lax.dot_general(potential, both_z, (((1,), (1,)), ((), ())), pr...  53.2 us
    slice x1, local copies, waits for them, and re-layouts, per_device(): sloped = sampled[:, :, 1]  43.7 us
    dot_general x1, matrix products, per_device(): lax.dot_general(potential, both_z, (((1,), (1,)), ((), ())), precision=HIGH)  32.4 us
    reduce_sum x1, other arithmetic, per_device(): jnp.sum(slope_x[:, None, :] * table_y[None, :, :] * plain, axis=(0, 1))  31.6 us
    all_to_all x2, waiting for transfers between devices, per_device(): spectrum = lax.all_to_all(spectrum, 'py', 0, 0, tiled=True)  28.1 us
    all_to_all x2, waiting for transfers between devices, per_device(): spectrum = lax.all_to_all(spectrum, 'px', 0, 0, tiled=True)  20.7 us
    add x1, other arithmetic, place_depth(): table + jnp.where(depth_index == ((base + k) % extent)[:, None], values[k...  19.9 us
    dot_general x1, matrix products, per_device(): jnp.einsum('dcilsy,sckxy->idlkx', turn_y, spectrum, precision=HIGH)  19 us
  transfers between devices with their start and end apart: 12, of which 11 were waited for; matrix products, arithmetic and copies ran while one was open for 5% of the time, Pallas kernels for 0%

commit v1 on v0

--- a/solution.py
+++ b/solution.py
@@ -323,18 +323,10 @@
     potential = jnp.einsum("zcjk,jckm->mz", back_z, spectrum, precision=HIGH)
     potential = potential.reshape(span_x, span_y, K)
     lower_rows = from_behind(potential[:5], "px", -1)
+    potential = jnp.concatenate([potential, lower_rows], axis=0)
     lower_cols = from_behind(potential[:, :5], "py", -1)
-    lower_corner = from_corner(potential[:5, :5], -1)
     gap = jnp.zeros((span_x + 5, pad_y - span_y - 5, K), jnp.float32)
-    potential = jnp.concatenate(
-        [
-            jnp.concatenate([potential, lower_rows], axis=0),
-            jnp.concatenate([lower_cols, lower_corner], axis=0),
-            gap,
-        ],
-        axis=1,
-    ).reshape(-1, K)
-    potential = lax.optimization_barrier(potential)
+    potential = jnp.concatenate([potential, lower_cols, gap], axis=1).reshape(-1, K)
 
     sampled = lax.dot_general(
         potential, both_z, (((1,), (1,)), ((), ())), precision=HIGH

time: 433 us -> 338 us (0.78)
  local copies, waits for them, and re-layouts: 144 us -> 47.3 us
  other arithmetic: 81.7 us -> 65 us
  matrix products: 82.3 us -> 97.4 us
  waiting for transfers between devices: 79.1 us -> 86.5 us
    reshape x1 -> x0, local copies, waits for them, and re-layouts: 53.2 us -> none  [per_device(): sampled = lax.dot_general(potential, both_z, (((1,), (1,)), ((), ())), pr...]
    slice x3 -> x0, local copies, waits for them, and re-layouts: 43.7 us -> none  [the longest x1 43.7 us: per_device(): sloped = sampled[:, :, 1]]
    reduce_sum x1, other arithmetic: 31.6 us -> 15.4 us  [per_device(): jnp.sum(table_x[:, None, :] * slope_y[None, :, :] * plain, axis=(0, 1))]
    dot_general x1, matrix products: 32.4 us -> 47.4 us  [per_device(): lax.dot_general(potential, both_z, (((1,), (1,)), ((), ())), precision=HIGH)]
    ppermute x4, waiting for transfers between devices: 9.45 us -> 19.9 us  [from_behind(): return lax.ppermute(value, axis, pairs)]
  transfers between devices with their start and end apart: 12 -> 11, of which waited for: 11 -> 11; matrix products, arithmetic and copies ran while one was open for 5% -> 6% of each run, Pallas kernels for 0% -> 0%
where the time goes in v1:
time: 338 us; the launch traced here: 332 us
  matrix products  97.4 us (29%)
  waiting for transfers between devices  86.5 us (26%)
  other arithmetic  65 us (19%)
  local copies, waits for them, and re-layouts  47.3 us (14%)
  starting transfers between devices  34.6 us (10%)
    dot_general x1, matrix products, per_device(): lax.dot_general(potential, both_z, (((1,), (1,)), ((), ())), precision=HIGH)  47.4 us
    all_to_all x2, waiting for transfers between devices, per_device(): spectrum = lax.all_to_all(spectrum, 'py', 0, 0, tiled=True)  28.5 us
    all_to_all x2, waiting for transfers between devices, per_device(): spectrum = lax.all_to_all(spectrum, 'px', 0, 0, tiled=True)  20.7 us
    add x1, other arithmetic, place_depth(): table + jnp.where(depth_index == ((base + k) % extent)[:, None], values[k...  20.3 us
    ppermute x4, waiting for transfers between devices, from_behind(): return lax.ppermute(value, axis, pairs)  19.9 us
    dot_general x1, matrix products, per_device(): jnp.einsum('dcilsy,sckxy->idlkx', turn_y, spectrum, precision=HIGH)  19.2 us
    reduce_sum x1, other arithmetic, per_device(): jnp.sum(table_x[:, None, :] * slope_y[None, :, :] * plain, axis=(0, 1))  15.4 us
    all_to_all x2, starting transfers between devices, per_device(): spectrum = lax.all_to_all(spectrum, 'px', 0, 0, tiled=True)  11 us
  transfers between devices with their start and end apart: 11, of which 11 were waited for; matrix products, arithmetic and copies ran while one was open for 6% of the time, Pallas kernels for 0%

profile of v1, /device:TPU:0, one launch (start us, length us, event | category | flops | bytes accessed | tf_op | source)
XLA Modules:
  0.0 332.5 jit_solution(6671471850234892140)
XLA Ops:
  7.1 7.1 %all-to-all-start = ((f32[16,3,5,128]{3,1,2,0:T(4,128)}), f32[16,3,5,128]{3,1,2,0:T(4,128)S(1)}, u32[]{:S(2)}, u32[]{:S(2)}) async-start(f32[16,3,5,128]{3,1,2,0:T(4,128)} %copy.59), calls=%async_computation | async-start | bytes 327680 | tf_op jit(solution)/shard_map/all_to_all | solution.py:257
  14.3 8.2 %all-to-all-done = f32[16,3,5,128]{3,1,2,0:T(4,128)S(1)} async-done(((f32[16,3,5,128]{3,1,2,0:T(4,128)}), f32[16,3,5,128]{3,1,2,0:T(4,128)S(1)}, u32[]{:S(2)}, u32[]{:S(2)}) %all-to-all-start) | async-done | bytes 122912 | tf_op jit(solution)/shard_map/all_to_all | solution.py:257
  23.2 20.3 %select_add_fusion = f32[12288,256]{1,0:T(8,128)S(1)} fusion(f32[12288]{0:T(1024)S(1)} %get-tuple-element.146, s32[12288]{0:T(1024)S(1)} %get-tuple-element.117, f32[12288]{0:T(1024)S(1)} %get-tuple-element.145, s32[12288]{0:T(1024)S(1)} %get-tuple-element.118, f32[12288]{0:T(1024)S(1)} %get-tuple-element.141, s32[12288]{0:T(1024)S(1)} %get-tuple-element.121, ...), kind=kLoop, calls=%fused_computation.10 | loop fusion | flops 53477376 | bytes 13172736 | tf_op jit(solution)/shard_map/add | solution.py:222
  47.8 8.8 %fusion.2 = f32[37,24,256]{2,1,0:T(8,128)S(1)} fusion(f32[37,6144]{1,0:T(8,128)S(1)} %get-tuple-element.61, f32[24,6144]{1,0:T(8,128)S(1)} %get-tuple-element.67, f32[12288,256]{1,0:T(8,128)S(1)} %select_add_fusion), kind=kOutput, calls=%fused_computation.8 | convolution fusion | flops 8385675264 | bytes 8773632 | tf_op jit(solution)/shard_map/dot_general | solution.py:280
  61.7 7.7 %collective-permute-done.1 = f32[32,5,256]{2,1,0:T(8,128)S(1)} collective-permute-done((f32[32,5,256]{2,1,0:T(8,128)S(1)}, f32[32,5,256]{2,1,0:T(8,128)S(1)}, u32[]{:S(2)}, u32[]{:S(2)}) %collective-permute-start.1) | collective-permute-done | bytes 163872 | tf_op jit(solution)/shard_map/ppermute | solution.py:31
  73.3 3.7 %all-to-all-start.1 = ((f32[16,2,16,512]{3,2,1,0:T(8,128)}), f32[16,2,16,512]{3,2,1,0:T(8,128)S(1)}, u32[]{:S(2)}, u32[]{:S(2)}) async-start(f32[16,2,16,512]{3,2,1,0:T(8,128)} %copy.61), calls=%async_computation.1 | async-start | bytes 2097152 | tf_op jit(solution)/shard_map/all_to_all | solution.py:297
  77.3 5.9 %fusion.69 = (f32[1,1,8,32,16,16]{3,5,4,1,2,0:T(8,128)S(1)}, f32[1,1,8,32,16,16]{3,5,4,1,2,0:T(8,128)}, f32[1,1,8,32,16,16]{3,5,4,1,2,0:T(8,128)}) fusion(s32[16,16]{1,0:T(8,128)S(1)} %multiply_add_fusion, s32[8,32]{1,0:T(8,128)S(1)} %multiply_add_fusion.1), kind=kLoop, calls=%fused_computation.116 | loop fusion | flops 983040 | bytes 788480 | tf_op jit(solution)/shard_map/sin | solution.py:96
  83.2 12.0 %all-to-all-done.1 = f32[16,2,16,512]{3,2,1,0:T(8,128)S(1)} async-done(((f32[16,2,16,512]{3,2,1,0:T(8,128)}), f32[16,2,16,512]{3,2,1,0:T(8,128)S(1)}, u32[]{:S(2)}, u32[]{:S(2)}) %all-to-all-start.1) | async-done | bytes 1048608 | tf_op jit(solution)/shard_map/all_to_all | solution.py:297
  95.2 4.9 %reshape.2975 = f32[16,2,16,32,16]{4,3,2,1,0:T(8,128)} reshape(f32[16,2,16,512]{3,2,1,0:T(8,128)S(1)} %all-to-all-done.1) | data formatting | bytes 2097152 | tf_op jit(solution)/shard_map/reshape | solution.py:298
  100.1 19.2 %fusion.27 = f32[8,2,32,16,32]{2,4,0,1,3:T(8,128)} fusion(f32[1,1,8,32,16,16]{3,5,4,1,2,0:T(8,128)} %get-tuple-element.124, f32[1,1,8,32,16,16]{3,5,4,1,2,0:T(8,128)} %get-tuple-element.123, f32[1,1,8,32,16,16]{3,5,4,1,2,0:T(8,128)S(1)} %get-tuple-element.122, f32[16,2,16,32,16]{4,3,2,1,0:T(8,128)} %reshape.2975), kind=kOutput, calls=%fused_computation.41 | convolution fusion | flops 806092800 | bytes 2883584 | tf_op jit(solution)/shard_map/dcilsy,sckxy->idlkx/dot_general | solution.py:300
  119.3 5.6 %copy.63 = f32[8,2,32,16,32]{4,3,2,1,0:T(8,128)} copy(f32[8,2,32,16,32]{2,4,0,1,3:T(8,128)} %fusion.27) | data formatting | bytes 2097152 | tf_op jit(solution)/shard_map/dcilsy,sckxy->idlkx/transpose | solution.py:300
  124.9 4.4 %reshape.2976 = f32[8,2,32,512]{3,2,1,0:T(8,128)} reshape(f32[8,2,32,16,32]{4,3,2,1,0:T(8,128)} %copy.63) | data formatting | bytes 2097152 | tf_op jit(solution)/shard_map/reshape | solution.py:301
  129.3 7.2 %all-to-all-start.2 = ((f32[8,2,32,512]{3,2,1,0:T(8,128)}), f32[8,2,32,512]{3,2,1,0:T(8,128)S(1)}, u32[]{:S(2)}, u32[]{:S(2)}) async-start(f32[8,2,32,512]{3,2,1,0:T(8,128)} %reshape.2976), calls=%async_computation.2 | async-start | bytes 2097152 | tf_op jit(solution)/shard_map/all_to_all | solution.py:302
  141.7 10.7 %all-to-all-done.2 = f32[8,2,32,512]{3,2,1,0:T(8,128)S(1)} async-done(((f32[8,2,32,512]{3,2,1,0:T(8,128)}), f32[8,2,32,512]{3,2,1,0:T(8,128)S(1)}, u32[]{:S(2)}, u32[]{:S(2)}) %all-to-all-start.2) | async-done | bytes 1048608 | tf_op jit(solution)/shard_map/all_to_all | solution.py:302
  153.3 3.0 reshape.3005
  156.2 4.5 %fusion.22 = f32[32,16,2,256,1,1]{3,1,4,2,0,5:T(8,128)S(1)} fusion(f32[8,2,32,16,32,1]{4,3,1,2,0,5:T(8,128)} %reshape.3005, f32[1,1,256,8,32]{2,4,3,1,0:T(8,128)} %get-tuple-element.134, f32[1,1,256,8,32]{2,4,3,1,0:T(8,128)} %get-tuple-element.133, f32[1,1,256,8,32]{2,4,3,1,0:T(8,128)} %get-tuple-element.132), kind=kOutput, calls=%fused_computation.38 | convolution fusion | flops 806092800 | bytes 2883584 | tf_op jit(solution)/shard_map/dcqrx,rclkx->qdlk/dot_general | solution.py:305
  160.8 5.0 %convolution_bitcast_fusion = f32[8,2,32,16,32]{4,3,0,1,2:T(8,128)} fusion(f32[1,1,8,32,256]{4,3,1,2,0:T(8,128)S(1)} %copy-done.7, f32[1,1,8,32,256]{4,3,1,2,0:T(8,128)S(1)} %copy-done.6, f32[1,1,8,32,256]{4,3,1,2,0:T(8,128)S(1)} %get-tuple-element.135, f32[32,16,2,256,1,1]{3,1,4,2,0,5:T(8,128)S(1)} %fusion.22, f32[256,32,16]{0,2,1:T(8,128)S(1)} %copy-done.5), kind=kOutput, calls=%fused_computation.42 | convolution fusion | flops 806354944 | bytes 3407872 | tf_op jit(solution)/shard_map/dcrxq,qclk->rdlkx/dot_general | solution.py:314
  165.8 3.5 %reshape.2978 = f32[8,2,32,512]{3,0,1,2:T(8,128)S(1)} reshape(f32[8,2,32,16,32]{4,3,0,1,2:T(8,128)} %convolution_bitcast_fusion) | data formatting | bytes 2097152 | tf_op jit(solution)/shard_map/reshape | solution.py:315
  170.9 3.8 %all-to-all-start.3 = ((f32[8,2,32,512]{3,2,1,0:T(8,128)}), f32[8,2,32,512]{3,2,1,0:T(8,128)S(1)}, u32[]{:S(2)}, u32[]{:S(2)}) async-start(f32[8,2,32,512]{3,2,1,0:T(8,128)} %copy.67), calls=%async_computation.3 | async-start | bytes 2097152 | tf_op jit(solution)/shard_map/all_to_all | solution.py:316
  174.7 5.8 %fusion.73 = (f32[1,1,16,16,8,32]{5,3,4,1,2,0:T(8,128)S(1)}, f32[1,1,16,16,8,32]{5,3,4,1,2,0:T(8,128)}, f32[1,1,16,16,8,32]{5,3,4,1,2,0:T(8,128)}) fusion(s32[8,32]{1,0:T(8,128)S(1)} %multiply_add_fusion.1, s32[16,16]{1,0:T(8,128)S(1)} %multiply_add_fusion), kind=kLoop, calls=%fused_computation.133 | loop fusion | flops 983040 | bytes 788480 | tf_op jit(solution)/shard_map/neg | solution.py:294
  180.6 10.0 %all-to-all-done.3 = f32[8,2,32,512]{3,2,1,0:T(8,128)S(1)} async-done(((f32[8,2,32,512]{3,2,1,0:T(8,128)}), f32[8,2,32,512]{3,2,1,0:T(8,128)S(1)}, u32[]{:S(2)}, u32[]{:S(2)}) %all-to-all-start.3) | async-done | bytes 1048608 | tf_op jit(solution)/shard_map/all_to_all | solution.py:316
  190.6 2.5 reshape.2979
  193.1 10.8 %fusion.24 = f32[16,2,16,32,16]{3,4,0,1,2:T(8,128)} fusion(f32[1,1,16,16,8,32]{5,3,4,1,2,0:T(8,128)} %get-tuple-element.127, f32[1,1,16,16,8,32]{5,3,4,1,2,0:T(8,128)} %get-tuple-element.126, f32[1,1,16,16,8,32]{5,3,4,1,2,0:T(8,128)S(1)} %get-tuple-element.125, f32[8,2,32,16,32,1,1]{4,3,2,1,0,6,5:T(8,128)} %bitcast.326), kind=kOutput, calls=%fused_computation.40 | convolution fusion | flops 806092800 | bytes 2883584 | tf_op jit(solution)/shard_map/dcsyil,iclkx->sdkxy/dot_general | solution.py:319
  203.9 7.0 %copy.69 = f32[16,2,16,32,16]{4,3,2,1,0:T(8,128)} copy(f32[16,2,16,32,16]{3,4,0,1,2:T(8,128)} %fusion.24) | data formatting | bytes 2097152 | tf_op jit(solution)/shard_map/dcsyil,iclkx->sdkxy/transpose | solution.py:319
  211.0 8.3 %reshape.2980 = f32[16,2,16,512]{3,2,1,0:T(8,128)} reshape(f32[16,2,16,32,16]{4,3,2,1,0:T(8,128)} %copy.69) | data formatting | bytes 2097152 | tf_op jit(solution)/shard_map/reshape | solution.py:320
  219.3 3.7 %all-to-all-start.4 = ((f32[16,2,16,512]{3,2,1,0:T(8,128)}), f32[16,2,16,512]{3,2,1,0:T(8,128)S(1)}, u32[]{:S(2)}, u32[]{:S(2)}) async-start(f32[16,2,16,512]{3,2,1,0:T(8,128)} %reshape.2980), calls=%async_computation.4 | async-start | bytes 2097152 | tf_op jit(solution)/shard_map/all_to_all | solution.py:321
  224.1 16.5 %all-to-all-done.4 = f32[16,2,16,512]{3,2,1,0:T(8,128)S(1)} async-done(((f32[16,2,16,512]{3,2,1,0:T(8,128)}), f32[16,2,16,512]{3,2,1,0:T(8,128)S(1)}, u32[]{:S(2)}, u32[]{:S(2)}) %all-to-all-start.4) | async-done | bytes 1048608 | tf_op jit(solution)/shard_map/all_to_all | solution.py:321
  244.7 8.9 %collective-permute-done.4 = f32[37,5,256]{2,1,0:T(8,128)S(1)} collective-permute-done((f32[37,5,256]{2,1,0:T(8,128)S(1)}, f32[37,5,256]{2,1,0:T(8,128)S(1)}, u32[]{:S(2)}, u32[]{:S(2)}) %collective-permute-start.4) | collective-permute-done | bytes 189472 | tf_op jit(solution)/shard_map/ppermute | solution.py:31
  253.7 47.4 %fusion.47 = f32[37,24,2,6144]{3,1,2,0:T(8,128)} fusion(f32[2,6144,256,1]{2,1,0,3:T(8,128)} %bitcast.325, f32[37,5,256]{2,1,0:T(8,128)S(1)} %collective-permute-done.4, f32[5,16,256]{2,1,0:T(8,128)S(1)} %collective-permute-done.3, f32[32,16,256]{2,1,0:T(8,128)S(1)} %bitcast.338, f32[24]{0:T(128)S(1)} %pad.14.clone), kind=kOutput, calls=%fused_computation.86 | convolution fusion | flops 16761120768 | bytes 57025632 | tf_op jit(solution)/shard_map/dot_general | solution.py:331
  301.1 15.4 %multiply_reduce_fusion = (f32[6144]{0:T(1024)S(1)}, f32[6144]{0:T(1024)S(1)}, f32[6144]{0:T(1024)S(1)}) fusion(f32[37,24,2,6144]{3,1,2,0:T(8,128)} %fusion.47, f32[24,6144]{1,0:T(8,128)S(1)} %copy-done.2, f32[37,6144]{1,0:T(8,128)S(1)} %get-tuple-element.60, f32[24,6144]{1,0:T(8,128)S(1)} %copy-done.4, f32[37,6144]{1,0:T(8,128)S(1)} %copy-done.1), kind=kLoop, calls=%fused_computation.6 | loop fusion | flops 49084416 | bytes 46718976 | tf_op jit(solution)/shard_map/reduce_sum | solution.py:337
  317.2 5.6 %all-to-all-start.5 = ((f32[16,3,3,128]{3,1,2,0:T(4,128)}), f32[16,3,3,128]{3,1,2,0:T(4,128)S(1)}, u32[]{:S(2)}, u32[]{:S(2)}) async-start(f32[16,3,3,128]{3,1,2,0:T(4,128)} %copy.72), calls=%async_computation.5 | async-start | bytes 196608 | tf_op jit(solution)/shard_map/all_to_all | solution.py:341
  322.9 7.8 %all-to-all-done.5 = f32[16,3,3,128]{3,1,2,0:T(4,128)S(1)} async-done(((f32[16,3,3,128]{3,1,2,0:T(4,128)}), f32[16,3,3,128]{3,1,2,0:T(4,128)S(1)}, u32[]{:S(2)}, u32[]{:S(2)}) %all-to-all-start.5) | async-done | bytes 73760 | tf_op jit(solution)/shard_map/all_to_all | solution.py:341
  (100 shorter events, 35.5 us)
Async XLA Ops:
  7.1 15.3 %all-to-all-start = ((f32[16,3,5,128]{3,1,2,0:T(4,128)}), f32[16,3,5,128]{3,1,2,0:T(4,128)S(1)}, u32[]{:S(2)}, u32[]{:S(2)}) async-start(f32[16,3,5,128]{3,1,2,0:T(4,128)} %copy.59), calls=%async_computation | async-start | bytes 327680 | tf_op jit(solution)/shard_map/all_to_all | solution.py:257
  43.4 13.1 %copy-start = (f32[12288,256]{1,0:T(8,128)}, f32[12288,256]{1,0:T(8,128)S(1)}, u32[]{:S(2)}) copy-start(f32[12288,256]{1,0:T(8,128)S(1)} %select_add_fusion) | copy-start | bytes 37748740
  45.3 11.3 %copy-start.3 = (f32[24,6144]{1,0:T(8,128)}, f32[24,6144]{1,0:T(8,128)S(1)}, u32[]{:S(2)}) copy-start(f32[24,6144]{1,0:T(8,128)S(1)} %get-tuple-element.67) | copy-start | bytes 1769476
  56.6 5.1 %collective-permute-start = (f32[5,16,256]{2,1,0:T(8,128)S(1)}, f32[5,16,256]{2,1,0:T(8,128)S(1)}, u32[]{:S(2)}, u32[]{:S(2)}) collective-permute-start(f32[5,16,256]{2,1,0:T(8,128)S(1)} %slice.158), channel_id=1, source_target_pairs={{0,16},{16,32},{32,48},{48,64},{64,80},{80,96},{96,112},{112,0},{1... | collective-permute-start | bytes 245768 | tf_op jit(solution)/shard_map/ppermute | solution.py:31
  57.9 11.5 %collective-permute-start.1 = (f32[32,5,256]{2,1,0:T(8,128)S(1)}, f32[32,5,256]{2,1,0:T(8,128)S(1)}, u32[]{:S(2)}, u32[]{:S(2)}) collective-permute-start(f32[32,5,256]{2,1,0:T(8,128)S(1)} %slice.160), channel_id=1, source_target_pairs={{0,1},{1,2},{2,3},{3,4},{4,5},{5,6},{6,7},{7,8},{8,9},{9,10},{10,1... | collective-permute-start | bytes 491528 | tf_op jit(solution)/shard_map/ppermute | solution.py:31
  58.5 12.9 %collective-permute-start.2 = (f32[5,5,256]{2,1,0:T(8,128)S(1)}, f32[5,5,256]{2,1,0:T(8,128)S(1)}, u32[]{:S(2)}, u32[]{:S(2)}) collective-permute-start(f32[5,5,256]{2,1,0:T(8,128)S(1)} %slice.162), channel_id=1, source_target_pairs={{0,17},{1,18},{2,19},{3,20},{4,21},{5,22},{6,23},{7,24},{8,25},{9,... | collective-permute-start | bytes 76808 | tf_op jit(solution)/shard_map/ppermute | solution.py:42
  73.3 21.9 %all-to-all-start.1 = ((f32[16,2,16,512]{3,2,1,0:T(8,128)}), f32[16,2,16,512]{3,2,1,0:T(8,128)S(1)}, u32[]{:S(2)}, u32[]{:S(2)}) async-start(f32[16,2,16,512]{3,2,1,0:T(8,128)} %copy.61), calls=%async_computation.1 | async-start | bytes 2097152 | tf_op jit(solution)/shard_map/all_to_all | solution.py:297
  129.3 23.1 %all-to-all-start.2 = ((f32[8,2,32,512]{3,2,1,0:T(8,128)}), f32[8,2,32,512]{3,2,1,0:T(8,128)S(1)}, u32[]{:S(2)}, u32[]{:S(2)}) async-start(f32[8,2,32,512]{3,2,1,0:T(8,128)} %reshape.2976), calls=%async_computation.2 | async-start | bytes 2097152 | tf_op jit(solution)/shard_map/all_to_all | solution.py:302
  153.2 7.5 %copy-start.5 = (f32[256,32,16]{0,2,1:T(8,128)S(1)}, f32[256,32,16]{0,2,1:T(8,128)}, u32[]{:S(2)}) copy-start(f32[256,32,16]{0,2,1:T(8,128)} %fusion.54) | copy-start | bytes 1572868
  153.2 7.5 %copy-start.6 = (f32[1,1,8,32,256]{4,3,1,2,0:T(8,128)S(1)}, f32[1,1,8,32,256]{4,3,1,2,0:T(8,128)}, u32[]{:S(2)}) copy-start(f32[1,1,8,32,256]{4,3,1,2,0:T(8,128)} %get-tuple-element.136) | copy-start | bytes 786436
  153.2 7.5 %copy-start.7 = (f32[1,1,8,32,256]{4,3,1,2,0:T(8,128)S(1)}, f32[1,1,8,32,256]{4,3,1,2,0:T(8,128)}, u32[]{:S(2)}) copy-start(f32[1,1,8,32,256]{4,3,1,2,0:T(8,128)} %get-tuple-element.137) | copy-start | bytes 786436
  170.9 19.7 %all-to-all-start.3 = ((f32[8,2,32,512]{3,2,1,0:T(8,128)}), f32[8,2,32,512]{3,2,1,0:T(8,128)S(1)}, u32[]{:S(2)}, u32[]{:S(2)}) async-start(f32[8,2,32,512]{3,2,1,0:T(8,128)} %copy.67), calls=%async_computation.3 | async-start | bytes 2097152 | tf_op jit(solution)/shard_map/all_to_all | solution.py:316
  211.0 33.8 %copy-start.8 = (s32[32,1]{0,1:T(1,128)S(1)}, s32[32,1]{0,1:T(1,128)}, u32[]{:S(2)}) copy-start(s32[32,1]{0,1:T(1,128)} %param.14) | copy-start | bytes 388
  219.3 21.3 %all-to-all-start.4 = ((f32[16,2,16,512]{3,2,1,0:T(8,128)}), f32[16,2,16,512]{3,2,1,0:T(8,128)S(1)}, u32[]{:S(2)}, u32[]{:S(2)}) async-start(f32[16,2,16,512]{3,2,1,0:T(8,128)} %reshape.2980), calls=%async_computation.4 | async-start | bytes 2097152 | tf_op jit(solution)/shard_map/all_to_all | solution.py:321
  241.6 2.1 collective-permute-start.3
  243.7 9.9 %collective-permute-start.4 = (f32[37,5,256]{2,1,0:T(8,128)S(1)}, f32[37,5,256]{2,1,0:T(8,128)S(1)}, u32[]{:S(2)}, u32[]{:S(2)}) collective-permute-start(f32[37,5,256]{2,1,0:T(8,128)S(1)} %pad_maximum_fusion), channel_id=1, source_target_pairs={{0,15},{1,0},{2,1},{3,2},{4,3},{5,4},{6,5},{7,6},{8,7},{9,8},{10,9... | collective-permute-start | bytes 568328 | tf_op jit(solution)/shard_map/ppermute | solution.py:31
  253.6 47.4 %copy-start.1 = (f32[37,6144]{1,0:T(8,128)S(1)}, f32[37,6144]{1,0:T(8,128)}, u32[]{:S(2)}) copy-start(f32[37,6144]{1,0:T(8,128)} %get-tuple-element.62) | copy-start | bytes 2727940
  253.7 47.4 %copy-start.2 = (f32[24,6144]{1,0:T(8,128)S(1)}, f32[24,6144]{1,0:T(8,128)}, u32[]{:S(2)}) copy-start(f32[24,6144]{1,0:T(8,128)} %get-tuple-element.66) | copy-start | bytes 1769476
  253.7 47.4 %copy-start.4 = (f32[24,6144]{1,0:T(8,128)S(1)}, f32[24,6144]{1,0:T(8,128)}, u32[]{:S(2)}) copy-start(f32[24,6144]{1,0:T(8,128)} %copy-done.3) | copy-start | bytes 1769476
  317.2 13.4 %all-to-all-start.5 = ((f32[16,3,3,128]{3,1,2,0:T(4,128)}), f32[16,3,3,128]{3,1,2,0:T(4,128)S(1)}, u32[]{:S(2)}, u32[]{:S(2)}) async-start(f32[16,3,3,128]{3,1,2,0:T(4,128)} %copy.72), calls=%async_computation.5 | async-start | bytes 196608 | tf_op jit(solution)/shard_map/all_to_all | solution.py:341
